TPU v7x, 128 devices: a whole 4x4x4 slice. The times are simulated.
128 devices in a mesh: grp: 4 (over x), tok: 32 (over z, y, core).
Axes of the slice: x: 4, y: 4, z: 4, core: 2. Of those that a mesh axis runs over, the one named last changes fastest.
Arguments:
- tokens: bfloat16 [16384, 2560], P(('grp', 'tok')), may hold values from -6 to 6
- input_gain: bfloat16 [2560], replicated, may hold values from 0.25 to 1.75
- query_down: bfloat16 [2560, 768], replicated, may hold values from -0.125 to 0.125
- query_gain: bfloat16 [768], replicated, may hold values from 0.25 to 1.75
- query_up: bfloat16 [768, 1920], replicated, may hold values from -0.21875 to 0.21875
- latent_down: bfloat16 [2560, 288], replicated, may hold values from -0.125 to 0.125
- latent_gain: bfloat16 [256], replicated, may hold values from 0.25 to 1.75
- key_up: bfloat16 [256, 1280], replicated, may hold values from -0.375 to 0.375
- value_up: bfloat16 [256, 1280], replicated, may hold values from -0.375 to 0.375
- output_weight: bfloat16 [1280, 2560], replicated, may hold values from -0.15625 to 0.15625
- post_gain: bfloat16 [2560], replicated, may hold values from 0.25 to 1.75
- gate_weight: bfloat16 [2560, 3200], P('tok', 'grp'), may hold values from -0.125 to 0.125
- up_weight: bfloat16 [2560, 3200], P('tok', 'grp'), may hold values from -0.125 to 0.125
- down_weight: bfloat16 [3200, 2560], P('grp', 'tok'), may hold values from -0.109375 to 0.109375
- cache_latents: bfloat16 [16, 4096, 288], P('grp', 'tok'), as said below
- prompt_latents: bfloat16 [8, 1024, 288], P(None, 'tok'), as said below
- cache_len: int32 [16], replicated, may hold values from 1 to 4096, 32768 in all
- prompt_len: int32 [8], replicated, may hold values from 1 to 1024, 4096 in all
- prompt_of: int32 [16], replicated, may hold values from 0 to 7
Outputs:
- layer_out: bfloat16 [16384, 2560], P(('grp', 'tok'))
- new_latents: bfloat16 [16384, 288], P(('grp', 'tok'))
Inputs may be any that keep to these rules, and one draw needn't show every extreme that they name: `cache_len`: some request has exactly 4096 live cached rows. `prompt_len`: some stored prompt has exactly 1024 live rows. `cache_latents`: rows past a request's live length are stored but never read. `prompt_latents`: rows past a prompt's live length are stored but never read.
All inputs are finite; a program needn't handle non-finite values.
Results may differ from a plain program's by a relative error of at most 0.02.
Values may be sent and summed in bfloat16 or wider, within the bound.
No kernel may reach another device: no remote copies, remote signals or barrier semaphores. Data moves between devices by JAX's collectives and lax.ppermute only.
A program may use at most 128 MiB of HBM per device.

v0:
```python
import jax
import jax.numpy as jnp
from jax import lax
from jax.sharding import PartitionSpec as P

KVR = 256
HEADS = 20
NOPE = 64
ROPE = 32
VDIM = 64
SPAN = 1024
EPSILON = 1e-06


def passed_along(block, axis, distance):
    devices = range(lax.axis_size(axis))
    route = [(i - distance, i) for i in devices if i - distance in devices]
    return lax.ppermute(block, axis, route)


def norm_rows(values, gain_vector):
    mean_square = jnp.mean(values * values, axis=-1, keepdims=True)
    return values * lax.rsqrt(mean_square + EPSILON) * gain_vector.astype(jnp.float32)


def rotate(values, positions):
    half_width = values.shape[-1] // 2
    frequency = 10000.0 ** (-jnp.arange(half_width, dtype=jnp.float32) / half_width)
    angles = positions.astype(jnp.float32)[:, None] * frequency[None, :]
    if values.ndim == 3:
        angles = angles[:, None, :]
    cosine = jnp.cos(angles)
    sine_part = jnp.sin(angles)
    leading = values[..., :half_width]
    trailing = values[..., half_width:]
    return jnp.concatenate(
        [leading * cosine - trailing * sine_part, trailing * cosine + leading * sine_part], axis=-1
    )


def attend_segment(
    softmax_state, queries, key_rows, lowers, limits, block_count, key_block, score_scale
):

    def fold_block(step_index, carried):
        running_max, running_sum, running_out = carried
        first_key = step_index * key_block
        key_piece = lax.dynamic_slice_in_dim(key_rows, first_key, key_block, 0)
        scores = (
            jnp.einsum("rw,kw->rk", queries, key_piece, preferred_element_type=jnp.float32)
            * score_scale
        )
        key_place = (first_key + jnp.arange(key_block, dtype=jnp.int32))[None, :]
        live_keys = jnp.logical_and(key_place >= lowers[:, None], key_place < limits[:, None])
        next_max = jnp.maximum(running_max, jnp.max(jnp.where(live_keys, scores, -1e30), axis=1))
        weights = jnp.where(live_keys, jnp.exp(scores - next_max[:, None]), 0.0)
        factor = jnp.exp(running_max - next_max)
        running_sum = running_sum * factor + jnp.sum(weights, axis=1)
        running_out = running_out * factor[:, None] + jnp.dot(
            weights.astype(jnp.bfloat16), key_piece[:, :KVR], preferred_element_type=jnp.float32
        )
        return (next_max, running_sum, running_out)

    return lax.fori_loop(0, block_count, fold_block, softmax_state)


def body(
    tokens,
    input_gain,
    query_down,
    query_gain,
    query_up,
    latent_down,
    latent_gain,
    key_up,
    value_up,
    output_weight,
    post_gain,
    gate_weight,
    up_weight,
    down_weight,
    cache_latents,
    prompt_latents,
    cache_len,
    prompt_len,
    prompt_of,
):
    group_index = lax.axis_index("grp")
    shard_index = lax.axis_index("tok")
    tok_dev = tokens.shape[0]
    tok_count = lax.axis_size("tok")
    group_requests = tok_dev * tok_count // SPAN
    local_request = shard_index % group_requests
    owner = group_index * group_requests + local_request
    offset = shard_index // group_requests * tok_dev
    within = offset + jnp.arange(tok_dev, dtype=jnp.int32)
    own_prompt = prompt_of[owner]
    prompt_live = prompt_len[own_prompt]
    cache_live = cache_len[owner]
    positions = prompt_live + cache_live + within
    normed = norm_rows(tokens.astype(jnp.float32), input_gain).astype(jnp.bfloat16)
    query_latent = norm_rows(
        jnp.dot(normed, query_down, preferred_element_type=jnp.float32), query_gain
    ).astype(jnp.bfloat16)
    query_full = jnp.dot(query_latent, query_up, preferred_element_type=jnp.float32).astype(
        jnp.bfloat16
    )
    query_full = lax.optimization_barrier(query_full).reshape(tok_dev, HEADS, NOPE + ROPE)
    absorbed = jnp.einsum(
        "thd,khd->thk",
        query_full[..., :NOPE],
        key_up.reshape(KVR, HEADS, NOPE),
        preferred_element_type=jnp.float32,
    )
    turned = rotate(query_full[..., NOPE:].astype(jnp.float32), positions)
    queries = jnp.concatenate([absorbed, turned], axis=-1).astype(jnp.bfloat16)
    latent_raw = jnp.dot(normed, latent_down, preferred_element_type=jnp.float32)
    new_latents = jnp.concatenate(
        [norm_rows(latent_raw[:, :KVR], latent_gain), rotate(latent_raw[:, KVR:], positions)],
        axis=-1,
    ).astype(jnp.bfloat16)
    latent_width = new_latents.shape[1]
    shards_back = SPAN // tok_dev
    earlier_pieces = []
    passing = new_latents
    for back in range(1, shards_back):
        passing = passed_along(passing, "tok", group_requests)
        earlier_pieces.insert(0, passing)
    span_rows = jnp.concatenate(earlier_pieces + [new_latents], axis=0)
    lead_rows = (shards_back - 1) * tok_dev
    span_lower = jnp.broadcast_to(lead_rows - offset, (tok_dev,))
    span_limit = lead_rows + 1 + jnp.arange(tok_dev, dtype=jnp.int32)
    cache_all, prompt_all = (
        lax.all_gather(cache_latents, "tok", axis=1, tiled=True),
        lax.all_gather(prompt_latents, "tok", axis=1, tiled=True),
    )
    cache_rows = lax.dynamic_index_in_dim(cache_all, local_request, 0, keepdims=False)
    prompt_rows = lax.dynamic_index_in_dim(prompt_all, own_prompt, 0, keepdims=False)
    query_rows = queries.reshape(tok_dev * HEADS, latent_width)
    row_count = tok_dev * HEADS
    score_scale = 1.0 / (NOPE + ROPE) ** 0.5
    softmax_state = (
        jnp.full((row_count,), -1e30, jnp.float32),
        jnp.zeros((row_count,), jnp.float32),
        jnp.zeros((row_count, KVR), jnp.float32),
    )
    no_lower = jnp.zeros((tok_dev,), jnp.int32)
    segments = (
        (prompt_rows, no_lower, jnp.broadcast_to(prompt_live, (tok_dev,))),
        (cache_rows, no_lower, jnp.broadcast_to(cache_live, (tok_dev,))),
        (span_rows, span_lower, span_limit),
    )
    for key_rows, token_lower, token_limit in segments:
        lowers = jnp.repeat(token_lower, HEADS)
        limits = jnp.repeat(token_limit, HEADS)
        key_block = min(512, key_rows.shape[0])
        block_count = key_rows.shape[0] // key_block
        softmax_state = attend_segment(
            softmax_state, query_rows, key_rows, lowers, limits, block_count, key_block, score_scale
        )
    running_max, running_sum, running_out = softmax_state
    latent_out = (
        (running_out / running_sum[:, None]).astype(jnp.bfloat16).reshape(tok_dev, HEADS, KVR)
    )
    heads_out = (
        jnp.einsum(
            "thk,khv->thv",
            latent_out,
            value_up.reshape(KVR, HEADS, VDIM),
            preferred_element_type=jnp.float32,
        )
        .astype(jnp.bfloat16)
        .reshape(tok_dev, HEADS * VDIM)
    )
    attended = jnp.dot(heads_out, output_weight, preferred_element_type=jnp.float32)
    residual = lax.optimization_barrier(
        (tokens.astype(jnp.float32) + attended).astype(jnp.bfloat16)
    )
    post_norm = norm_rows(residual.astype(jnp.float32), post_gain).astype(jnp.bfloat16)
    rows_all = lax.all_gather(post_norm, "grp", axis=0, tiled=True)
    gate_values = jnp.dot(
        rows_all,
        lax.all_gather(gate_weight, "tok", axis=0, tiled=True),
        preferred_element_type=jnp.float32,
    )
    up_values = jnp.dot(
        rows_all,
        lax.all_gather(up_weight, "tok", axis=0, tiled=True),
        preferred_element_type=jnp.float32,
    )
    hidden = (jax.nn.silu(gate_values) * up_values).astype(jnp.bfloat16)
    partial_out = jnp.dot(
        hidden,
        lax.all_gather(down_weight, "tok", axis=1, tiled=True),
        preferred_element_type=jnp.float32,
    )
    down_values = lax.psum_scatter(
        partial_out.astype(jnp.bfloat16), "grp", scatter_dimension=0, tiled=True
    ).astype(jnp.float32)
    layer_out = (residual.astype(jnp.float32) + down_values).astype(jnp.bfloat16)
    return (layer_out, new_latents)


def solution(mesh):
    in_specs = (
        P(("grp", "tok"), None),
        P(),
        P(),
        P(),
        P(),
        P(),
        P(),
        P(),
        P(),
        P(),
        P(),
        P("tok", "grp"),
        P("tok", "grp"),
        P("grp", "tok"),
        P("grp", "tok", None),
        P(None, "tok", None),
        P(),
        P(),
        P(),
    )
    out_specs = (P(("grp", "tok"), None), P(("grp", "tok"), None))
    return jax.shard_map(body, mesh=mesh, in_specs=in_specs, out_specs=out_specs, check_vma=False)
```

profile of v0, /device:TPU:1, one launch (start us, length us, event | category | flops | bytes accessed | tf_op | source)
XLA Modules:
  0.0 412.8 jit_solution(16430526760427926107)
XLA Ops:
  20.9 6.3 %collective-permute-start = (bf16[128,288]{0,1:T(8,128)(2,1)S(1)}, bf16[128,288]{0,1:T(8,128)(2,1)}, u32[]{:S(2)}, u32[]{:S(2)}) collective-permute-start(bf16[128,288]{0,1:T(8,128)(2,1)S(1)} %pad_maximum_fusion.1), channel_id=1, source_target_pairs={{0,4},{1,5},{2,6},{3,7},{4,8},{5,9},{6,10},{7,11},{8,12},{9,13},{1... | collective-permute-start | bytes 221192 | tf_op jit(solution)/shard_map/ppermute | solution.py:18
  30.4 3.7 collective-permute-start.1
  36.4 4.5 %collective-permute-start.2 = (bf16[128,288]{0,1:T(8,128)(2,1)}, bf16[128,288]{0,1:T(8,128)(2,1)S(1)}, u32[]{:S(2)}, u32[]{:S(2)}) collective-permute-start(bf16[128,288]{0,1:T(8,128)(2,1)} %collective-permute-done.1), channel_id=1, source_target_pairs={{0,4},{1,5},{2,6},{3,7},{4,8},{5,9},{6,10},{7,11},{8,12},{9,13},{1... | collective-permute-start | bytes 221192 | tf_op jit(solution)/shard_map/ppermute | solution.py:18
  42.6 5.1 %collective-permute-start.3 = (bf16[128,288]{0,1:T(8,128)(2,1)S(1)}, bf16[128,288]{0,1:T(8,128)(2,1)S(1)}, u32[]{:S(2)}, u32[]{:S(2)}) collective-permute-start(bf16[128,288]{0,1:T(8,128)(2,1)S(1)} %collective-permute-done.2), channel_id=1, source_target_pairs={{0,4},{1,5},{2,6},{3,7},{4,8},{5,9},{6,10},{7,11},{8,12},{9,13},{1... | collective-permute-start | bytes 221192 | tf_op jit(solution)/shard_map/ppermute | solution.py:18
  50.7 5.6 %collective-permute-start.4 = (bf16[128,288]{0,1:T(8,128)(2,1)S(1)}, bf16[128,288]{0,1:T(8,128)(2,1)S(1)}, u32[]{:S(2)}, u32[]{:S(2)}) collective-permute-start(bf16[128,288]{0,1:T(8,128)(2,1)S(1)} %collective-permute-done.3), channel_id=1, source_target_pairs={{0,4},{1,5},{2,6},{3,7},{4,8},{5,9},{6,10},{7,11},{8,12},{9,13},{1... | collective-permute-start | bytes 221192 | tf_op jit(solution)/shard_map/ppermute | solution.py:18
  62.0 6.0 %collective-permute-start.5 = (bf16[128,288]{0,1:T(8,128)(2,1)S(1)}, bf16[128,288]{0,1:T(8,128)(2,1)S(1)}, u32[]{:S(2)}, u32[]{:S(2)}) collective-permute-start(bf16[128,288]{0,1:T(8,128)(2,1)S(1)} %collective-permute-done.4), channel_id=1, source_target_pairs={{0,4},{1,5},{2,6},{3,7},{4,8},{5,9},{6,10},{7,11},{8,12},{9,13},{1... | collective-permute-start | bytes 221192 | tf_op jit(solution)/shard_map/ppermute | solution.py:18
  87.5 26.8 %while.56 = (s32[]{:T(128)}, f32[2560]{0:T(1024)S(1)}, f32[2560]{0:T(1024)S(1)}, f32[2560,256]{1,0:T(8,128)S(1)}, bf16[1024,288]{1,0:T(8,128)(2,1)}, /*index=5*/...) while((s32[]{:T(128)}, f32[2560]{0:T(1024)S(1)}, ...), condition=%wide.region_5.6_spmd.clone, body=%wide.region_2.5_spmd.clone.sunk | while | flops 1439840768 | bytes 44730576 | solution.py:64
  88.0 5.6 %fusion.130 = (f32[2560]{0:T(1024)S(1)}, f32[512,2560]{1,0:T(8,128)}) fusion(pred[512]{0:T(512)(128)(4,1)S(1)} %fusion.129, bf16[2560,288]{1,0:T(8,128)(2,1)} %get-tuple-element.733, bf16[1024,288]{1,0:T(8,128)(2,1)} %get-tuple-element.732, s32[]{:T(128)S(6)} %select_n.152), kind=kOutput, calls=%fused_computation.53.clone.1 | convolution fusion | flops 758904320 | bytes 7612932 | tf_op jit(solution)/shard_map/while/body/eval_jaxpr/rw,kw->rk/dot_general | solution.py:50
  93.6 3.5 fusion.131
  101.1 5.6 %fusion.130 = (f32[2560]{0:T(1024)S(1)}, f32[512,2560]{1,0:T(8,128)}) fusion(pred[512]{0:T(512)(128)(4,1)S(1)} %fusion.129, bf16[2560,288]{1,0:T(8,128)(2,1)} %get-tuple-element.733, bf16[1024,288]{1,0:T(8,128)(2,1)} %get-tuple-element.732, s32[]{:T(128)S(6)} %select_n.152), kind=kOutput, calls=%fused_computation.53.clone.1 | convolution fusion | flops 758904320 | bytes 7612932 | tf_op jit(solution)/shard_map/while/body/eval_jaxpr/rw,kw->rk/dot_general | solution.py:50
  106.8 3.5 fusion.131
  114.3 14.3 %all-gather.9.cloned.1.call-done = bf16[4,4096,288]{1,2,0:T(8,128)(2,1)} async-done(((bf16[4,128,288]{1,2,0:T(8,128)(2,1)}), bf16[4,4096,288]{1,2,0:T(8,128)(2,1)}) %all-gather.9.cloned.1.call-update) | async-done | bytes 9437200 | tf_op jit(solution)/shard_map/all_gather | solution.py:134
  131.9 4.5 %copy.36 = bf16[1,4096,288]{2,1,0:T(8,128)(2,1)} copy(bf16[1,4096,288]{1,2,0:T(8,128)(2,1)} %constant_dynamic-slice_fusion) | data formatting | bytes 4718592 | tf_op jit(solution)/shard_map/jit(dynamic_index_in_dim)/dynamic_slice | solution.py:137
  136.4 61.9 %while.54 = (s32[]{:T(128)}, f32[2560]{0:T(1024)S(1)}, f32[2560]{0:T(1024)S(1)}, f32[2560,256]{1,0:T(8,128)S(1)}, bf16[4096,288]{1,0:T(8,128)(2,1)}, /*index=5*/...) while((s32[]{:T(128)}, f32[2560]{0:T(1024)S(1)}, ...), condition=%wide.region_9.10_spmd.clone, body=%wide.region_6.9_spmd.clone.sunk | while | flops 1439177728 | bytes 23759020 | solution.py:64
  198.3 19.1 %while.55 = (s32[]{:T(128)}, f32[2560]{0:T(1024)S(1)}, f32[2560]{0:T(1024)S(1)}, f32[2560,256]{1,0:T(8,128)S(1)}, bf16[1024,288]{0,1:T(8,128)(2,1)}, /*index=5*/...) while((s32[]{:T(128)}, f32[2560]{0:T(1024)S(1)}, ...), condition=%wide.region_14.15_spmd.clone, body=%wide.region_11.14_spmd.clone.sunk | while | flops 1447041536 | bytes 23730872 | solution.py:64
  198.7 4.0 fusion.124
  208.2 4.0 fusion.124
  221.9 3.9 fusion.59
  228.6 32.8 %all-gather.11.cloned.1.call-done = bf16[512,2560]{1,0:T(8,128)(2,1)} async-done(((bf16[128,2560]{1,0:T(8,128)(2,1)}), bf16[512,2560]{1,0:T(8,128)(2,1)}) %all-gather.11.cloned.1.call-update) | async-done | bytes 2621456 | tf_op jit(solution)/shard_map/all_gather | solution.py:180
  261.4 6.7 %fusion.81 = f32[512,800]{0,1:T(8,128)} fusion(bf16[512,2560]{1,0:T(8,128)(2,1)} %all-gather.11.cloned.1.call-done, bf16[2560,800]{1,0:T(8,128)(2,1)} %all-gather.13.cloned.1.call-done), kind=kOutput, calls=%fused_computation.136 | convolution fusion | flops 2097152000 | bytes 8355840 | tf_op jit(solution)/shard_map/dot_general | solution.py:181
  268.1 42.8 %all-gather.15.cloned.1.call-done = bf16[2560,800]{1,0:T(8,128)(2,1)} async-done(((bf16[80,800]{1,0:T(8,128)(2,1)}), bf16[2560,800]{1,0:T(8,128)(2,1)}) %all-gather.15.cloned.1.call-update) | async-done | bytes 4096016 | tf_op jit(solution)/shard_map/all_gather | solution.py:188
  310.9 48.1 %all-gather.17.cloned.1.call-done = bf16[800,2560]{0,1:T(8,128)(2,1)} async-done(((bf16[800,80]{0,1:T(8,128)(2,1)}), bf16[800,2560]{0,1:T(8,128)(2,1)}) %all-gather.17.cloned.1.call-update) | async-done | bytes 4096016 | tf_op jit(solution)/shard_map/all_gather | solution.py:194
  358.9 11.8 %convolution_convert_fusion = bf16[512,2560]{1,0:T(8,128)(2,1)} fusion(bf16[800,2560]{0,1:T(8,128)(2,1)} %all-gather.17.cloned.1.call-done, f32[512,800]{0,1:T(8,128)} %fusion.81, bf16[512,2560]{1,0:T(8,128)(2,1)} %all-gather.11.cloned.1.call-done, bf16[2560,800]{1,0:T(8,128)(2,1)} %all-gather.15.cloned.1.call-done), kind=kOutput, calls=%fused_computation.77 | convolution fusion | flops 4198072320 | bytes 15073280 | tf_op jit(solution)/shard_map/dot_general | solution.py:192
  370.7 32.9 %reduce-scatter.2.cloned.1.call-done = bf16[128,2560]{1,0:T(8,128)(2,1)} async-done(((bf16[512,2560]{1,0:T(8,128)(2,1)}), bf16[128,2560]{1,0:T(8,128)(2,1)}) %reduce-scatter.2.cloned.1.call-update) | async-done | bytes 655376 | tf_op jit(solution)/shard_map/reduce_scatter | solution.py:197
  (184 shorter events, 139.1 us)
Async XLA Ops:
  7.2 26.9 %copy-start = (bf16[768,1920]{1,0:T(8,128)(2,1)S(1)}, bf16[768,1920]{1,0:T(8,128)(2,1)}, u32[]{:S(2)}) copy-start(bf16[768,1920]{1,0:T(8,128)(2,1)} %param.29) | copy-start | bytes 8847364
  7.2 78.2 %all-gather.7.cloned.1.call-start = ((), (), s32[]{:S(2)}) async-start(), calls=%async_computation.1 | async-start | bytes 6488064 | tf_op jit(solution)/shard_map/all_gather | solution.py:135
  7.9 120.7 %all-gather.9.cloned.1.call-start = ((), (), s32[]{:S(2)}) async-start(), calls=%async_computation.2 | async-start | bytes 9732096 | tf_op jit(solution)/shard_map/all_gather | solution.py:134
  8.7 219.9 %all-gather.13.cloned.1.call-start = ((), (), s32[]{:S(2)}) async-start(), calls=%async_computation.4 | async-start | bytes 4730880 | tf_op jit(solution)/shard_map/all_gather | solution.py:183
  20.8 9.6 %copy-start.8 = (bf16[768]{0:T(1024)(128)(2,1)S(1)}, bf16[768]{0:T(1024)(128)(2,1)}, u32[]{:S(2)}) copy-start(bf16[768]{0:T(1024)(128)(2,1)} %param.28) | copy-start | bytes 4612
  20.8 13.3 %copy-start.6 = (bf16[128,288]{0,1:T(8,128)(2,1)}, bf16[128,288]{0,1:T(8,128)(2,1)S(1)}, u32[]{:S(2)}) copy-start(bf16[128,288]{0,1:T(8,128)(2,1)S(1)} %pad_maximum_fusion.1) | copy-start | bytes 221188
  20.9 9.6 %collective-permute-start = (bf16[128,288]{0,1:T(8,128)(2,1)S(1)}, bf16[128,288]{0,1:T(8,128)(2,1)}, u32[]{:S(2)}, u32[]{:S(2)}) collective-permute-start(bf16[128,288]{0,1:T(8,128)(2,1)S(1)} %pad_maximum_fusion.1), channel_id=1, source_target_pairs={{0,4},{1,5},{2,6},{3,7},{4,8},{5,9},{6,10},{7,11},{8,12},{9,13},{1... | collective-permute-start | bytes 221192 | tf_op jit(solution)/shard_map/ppermute | solution.py:18
  27.1 234.2 %all-gather.11.cloned.1.call-start = ((), (), s32[]{:S(2)}) async-start(), calls=%async_computation.3 | async-start | bytes 3276800 | tf_op jit(solution)/shard_map/all_gather | solution.py:180
  30.4 5.9 %collective-permute-start.1 = (bf16[128,288]{0,1:T(8,128)(2,1)}, bf16[128,288]{0,1:T(8,128)(2,1)}, u32[]{:S(2)}, u32[]{:S(2)}) collective-permute-start(bf16[128,288]{0,1:T(8,128)(2,1)} %collective-permute-done), channel_id=1, source_target_pairs={{0,4},{1,5},{2,6},{3,7},{4,8},{5,9},{6,10},{7,11},{8,12},{9,13},{1... | collective-permute-start | bytes 221192 | tf_op jit(solution)/shard_map/ppermute | solution.py:18
  36.4 6.2 %collective-permute-start.2 = (bf16[128,288]{0,1:T(8,128)(2,1)}, bf16[128,288]{0,1:T(8,128)(2,1)S(1)}, u32[]{:S(2)}, u32[]{:S(2)}) collective-permute-start(bf16[128,288]{0,1:T(8,128)(2,1)} %collective-permute-done.1), channel_id=1, source_target_pairs={{0,4},{1,5},{2,6},{3,7},{4,8},{5,9},{6,10},{7,11},{8,12},{9,13},{1... | collective-permute-start | bytes 221192 | tf_op jit(solution)/shard_map/ppermute | solution.py:18
  42.6 8.1 %collective-permute-start.3 = (bf16[128,288]{0,1:T(8,128)(2,1)S(1)}, bf16[128,288]{0,1:T(8,128)(2,1)S(1)}, u32[]{:S(2)}, u32[]{:S(2)}) collective-permute-start(bf16[128,288]{0,1:T(8,128)(2,1)S(1)} %collective-permute-done.2), channel_id=1, source_target_pairs={{0,4},{1,5},{2,6},{3,7},{4,8},{5,9},{6,10},{7,11},{8,12},{9,13},{1... | collective-permute-start | bytes 221192 | tf_op jit(solution)/shard_map/ppermute | solution.py:18
  50.7 11.3 %collective-permute-start.4 = (bf16[128,288]{0,1:T(8,128)(2,1)S(1)}, bf16[128,288]{0,1:T(8,128)(2,1)S(1)}, u32[]{:S(2)}, u32[]{:S(2)}) collective-permute-start(bf16[128,288]{0,1:T(8,128)(2,1)S(1)} %collective-permute-done.3), channel_id=1, source_target_pairs={{0,4},{1,5},{2,6},{3,7},{4,8},{5,9},{6,10},{7,11},{8,12},{9,13},{1... | collective-permute-start | bytes 221192 | tf_op jit(solution)/shard_map/ppermute | solution.py:18
  62.0 11.2 %copy-start.7 = (bf16[2560]{0:T(1024)(128)(2,1)S(1)}, bf16[2560]{0:T(1024)(128)(2,1)}, u32[]{:S(2)}) copy-start(bf16[2560]{0:T(1024)(128)(2,1)} %param.35) | copy-start | bytes 15364
  62.0 11.2 %collective-permute-start.5 = (bf16[128,288]{0,1:T(8,128)(2,1)S(1)}, bf16[128,288]{0,1:T(8,128)(2,1)S(1)}, u32[]{:S(2)}, u32[]{:S(2)}) collective-permute-start(bf16[128,288]{0,1:T(8,128)(2,1)S(1)} %collective-permute-done.4), channel_id=1, source_target_pairs={{0,4},{1,5},{2,6},{3,7},{4,8},{5,9},{6,10},{7,11},{8,12},{9,13},{1... | collective-permute-start | bytes 221192 | tf_op jit(solution)/shard_map/ppermute | solution.py:18
  73.1 5.2 %collective-permute-start.6 = (bf16[128,288]{0,1:T(8,128)(2,1)S(1)}, bf16[128,288]{0,1:T(8,128)(2,1)S(1)}, u32[]{:S(2)}, u32[]{:S(2)}) collective-permute-start(bf16[128,288]{0,1:T(8,128)(2,1)S(1)} %collective-permute-done.5), channel_id=1, source_target_pairs={{0,4},{1,5},{2,6},{3,7},{4,8},{5,9},{6,10},{7,11},{8,12},{9,13},{1... | collective-permute-start | bytes 221192 | tf_op jit(solution)/shard_map/ppermute | solution.py:18
  93.6 4.0 copy-start.2
  106.8 4.7 %copy-start.2 = (f32[512,2560]{1,0:T(8,128)S(1)}, f32[512,2560]{1,0:T(8,128)}, u32[]{:S(2)}) copy-start(f32[512,2560]{1,0:T(8,128)} %get-tuple-element.703) | copy-start | bytes 15728644 | tf_op jit(solution)/shard_map/while
  218.9 2.3 copy-start.5
  218.9 2.9 copy-start.4
  225.8 42.3 %copy-start.3 = (bf16[128,2560]{1,0:T(8,128)(2,1)}, bf16[128,2560]{1,0:T(8,128)(2,1)S(1)}, u32[]{:S(2)}) copy-start(bf16[128,2560]{1,0:T(8,128)(2,1)S(1)} %fusion.59) | copy-start | bytes 1966084
  227.1 83.7 %all-gather.15.cloned.1.call-start = ((), (), s32[]{:S(2)}) async-start(), calls=%async_computation.5 | async-start | bytes 4730880 | tf_op jit(solution)/shard_map/all_gather | solution.py:188
  227.7 131.2 %all-gather.17.cloned.1.call-start = ((), (), s32[]{:S(2)}) async-start(), calls=%async_computation.6 | async-start | bytes 4730880 | tf_op jit(solution)/shard_map/all_gather | solution.py:194
  228.3 175.4 %reduce-scatter.2.cloned.1.call-start = ((), (), s32[]{:S(2)}) async-start(), calls=%async_computation.7 | async-start | bytes 3276800 | tf_op jit(solution)/shard_map/reduce_scatter | solution.py:197
  358.9 47.0 %copy-start.1 = (bf16[768,1920]{1,0:T(8,128)(2,1)S(1)}, bf16[768,1920]{1,0:T(8,128)(2,1)}, u32[]{:S(2)}) copy-start(bf16[768,1920]{1,0:T(8,128)(2,1)} %param.29) | copy-start | bytes 8847364
Sparse Core Ops, SparseCore 0:
  10.3 55.2 all-gather.6
  67.7 60.8 all-gather.8
  130.9 46.1 all-gather.12
  227.2 34.1 all-gather.10
  263.6 47.2 all-gather.14
  313.0 45.8 all-gather.16
  370.9 32.7 reduce-scatter.1
where the time goes:
time: 415 us; the launch traced here: 413 us
  waiting for transfers between devices  179 us (43%)
  matrix products  109 us (26%)
  other arithmetic  37.2 us (9%)
  starting transfers between devices  35.1 us (8%)
  local copies, waits for them, and re-layouts  33.7 us (8%)
  between operations  17.6 us (4%)
    all_gather x1, waiting for transfers between devices, body(): lax.all_gather(down_weight, 'tok', axis=1, tiled=True)  48.1 us
    dot_general x12, matrix products, fold_block(): jnp.einsum('rw,kw->rk', queries, key_piece, preferred_element_type=jnp.fl...  45.9 us
    all_gather x1, waiting for transfers between devices, body(): lax.all_gather(up_weight, 'tok', axis=0, tiled=True)  42.8 us
    ppermute x7, starting transfers between devices, passed_along(): return lax.ppermute(block, axis, route)  34.6 us
    dot_general x12, matrix products, fold_block(): jnp.dot(weights.astype(jnp.bfloat16), key_piece[:, :KVR], preferred_eleme...  33.7 us
    reduce_scatter x1, waiting for transfers between devices, body(): lax.psum_scatter(partial_out.astype(jnp.bfloat16), 'grp', scatter_dimensi...  32.9 us
    all_gather x1, waiting for transfers between devices, body(): rows_all = lax.all_gather(post_norm, 'grp', axis=0, tiled=True)  32.8 us
    reduce_sum x12, other arithmetic, fold_block(): running_sum = running_sum * factor + jnp.sum(weights, axis=1)  19 us
  transfers between devices with their start and end apart: 14, of which 8 were waited for; matrix products, arithmetic and copies ran while one was open for 40% of the time, Pallas kernels for 0%

commit v1 on v0

--- a/solution.py
+++ b/solution.py
@@ -10,6 +10,19 @@
 VDIM = 64
 SPAN = 1024
 EPSILON = 1e-06
+
+
+def collect(value, axis, dim):
+    ways = lax.axis_size(axis)
+    up = [(d, (d + 1) % ways) for d in range(ways)]
+    down = [(d, (d - 1) % ways) for d in range(ways)]
+    earlier, later = ([value], [value])
+    for _ in range(ways // 2):
+        earlier.append(lax.ppermute(earlier[-1], axis, up))
+    for _ in range((ways - 1) // 2):
+        later.append(lax.ppermute(later[-1], axis, down))
+    line = jnp.concatenate([*earlier[::-1], *later[1:]], axis=dim)
+    return jnp.roll(line, (lax.axis_index(axis) - ways // 2) * value.shape[dim], axis=dim)
 
 
 def passed_along(block, axis, distance):
@@ -177,7 +190,7 @@
         (tokens.astype(jnp.float32) + attended).astype(jnp.bfloat16)
     )
     post_norm = norm_rows(residual.astype(jnp.float32), post_gain).astype(jnp.bfloat16)
-    rows_all = lax.all_gather(post_norm, "grp", axis=0, tiled=True)
+    rows_all = collect(post_norm, "grp", 0)
     gate_values = jnp.dot(
         rows_all,
         lax.all_gather(gate_weight, "tok", axis=0, tiled=True),

time: 415 us -> 332 us (0.80)
  waiting for transfers between devices: 179 us -> 83.7 us
  local copies, waits for them, and re-layouts: 33.7 us -> 38.6 us
  starting transfers between devices: 35.1 us -> 39.4 us
    all_gather x1, waiting for transfers between devices: 48.1 us -> 0.01 us  [body(): lax.all_gather(down_weight, 'tok', axis=1, tiled=True)]
    all_gather x1, waiting for transfers between devices: 42.8 us -> 0.01 us  [body(): lax.all_gather(up_weight, 'tok', axis=0, tiled=True)]
    all_gather x1 -> x0, waiting for transfers between devices: 32.8 us -> none  [body(): rows_all = lax.all_gather(post_norm, 'grp', axis=0, tiled=True)]
    ppermute x0 -> x3, waiting for transfers between devices: none -> 29.7 us  [the longest x2 29.7 us: collect(): earlier.append(lax.ppermute(earlier[-1], axis, up))]
    unnamed x25 -> x32, local copies, waits for them, and re-layouts: 9.84 us -> 14.2 us
  transfers between devices with their start and end apart: 14 -> 16, of which waited for: 8 -> 7; matrix products, arithmetic and copies ran while one was open for 40% -> 52% of each run, Pallas kernels for 0% -> 0%
where the time goes in v1:
time: 332 us; the launch traced here: 330 us
  matrix products  109 us (33%)
  waiting for transfers between devices  83.7 us (25%)
  other arithmetic  39.8 us (12%)
  starting transfers between devices  39.4 us (12%)
  local copies, waits for them, and re-layouts  38.6 us (12%)
  between operations  17.8 us (5%)
    dot_general x12, matrix products, fold_block(): jnp.einsum('rw,kw->rk', queries, key_piece, preferred_element_type=jnp.fl...  46.1 us
    ppermute x7, starting transfers between devices, passed_along(): return lax.ppermute(block, axis, route)  35.2 us
    dot_general x12, matrix products, fold_block(): jnp.dot(weights.astype(jnp.bfloat16), key_piece[:, :KVR], preferred_eleme...  33.7 us
    reduce_scatter x1, waiting for transfers between devices, body(): lax.psum_scatter(partial_out.astype(jnp.bfloat16), 'grp', scatter_dimensi...  32.6 us
    ppermute x2, waiting for transfers between devices, collect(): earlier.append(lax.ppermute(earlier[-1], axis, up))  29.7 us
    reduce_sum x12, other arithmetic, fold_block(): running_sum = running_sum * factor + jnp.sum(weights, axis=1)  19.6 us
    unnamed x32, local copies, waits for them, and re-layouts  14.2 us
    all_gather x1, waiting for transfers between devices, body(): lax.all_gather(cache_latents, 'tok', axis=1, tiled=True)  12.7 us
  transfers between devices with their start and end apart: 16, of which 7 were waited for; matrix products, arithmetic and copies ran while one was open for 52% of the time, Pallas kernels for 0%

profile of v1, /device:TPU:1, one launch (start us, length us, event | category | flops | bytes accessed | tf_op | source)
XLA Modules:
  0.0 329.7 jit_solution(16423033308081365565)
XLA Ops:
  22.5 6.3 %collective-permute-start = (bf16[128,288]{0,1:T(8,128)(2,1)S(1)}, bf16[128,288]{0,1:T(8,128)(2,1)}, u32[]{:S(2)}, u32[]{:S(2)}) collective-permute-start(bf16[128,288]{0,1:T(8,128)(2,1)S(1)} %pad_maximum_fusion.1), channel_id=1, source_target_pairs={{0,4},{1,5},{2,6},{3,7},{4,8},{5,9},{6,10},{7,11},{8,12},{9,13},{1... | collective-permute-start | bytes 221192 | tf_op jit(solution)/shard_map/ppermute | solution.py:31
  32.0 4.5 %collective-permute-start.1 = (bf16[128,288]{0,1:T(8,128)(2,1)}, bf16[128,288]{0,1:T(8,128)(2,1)}, u32[]{:S(2)}, u32[]{:S(2)}) collective-permute-start(bf16[128,288]{0,1:T(8,128)(2,1)} %collective-permute-done), channel_id=1, source_target_pairs={{0,4},{1,5},{2,6},{3,7},{4,8},{5,9},{6,10},{7,11},{8,12},{9,13},{1... | collective-permute-start | bytes 221192 | tf_op jit(solution)/shard_map/ppermute | solution.py:31
  38.8 4.0 %collective-permute-start.2 = (bf16[128,288]{0,1:T(8,128)(2,1)}, bf16[128,288]{0,1:T(8,128)(2,1)S(1)}, u32[]{:S(2)}, u32[]{:S(2)}) collective-permute-start(bf16[128,288]{0,1:T(8,128)(2,1)} %collective-permute-done.1), channel_id=1, source_target_pairs={{0,4},{1,5},{2,6},{3,7},{4,8},{5,9},{6,10},{7,11},{8,12},{9,13},{1... | collective-permute-start | bytes 221192 | tf_op jit(solution)/shard_map/ppermute | solution.py:31
  44.5 5.1 %collective-permute-start.3 = (bf16[128,288]{0,1:T(8,128)(2,1)S(1)}, bf16[128,288]{0,1:T(8,128)(2,1)S(1)}, u32[]{:S(2)}, u32[]{:S(2)}) collective-permute-start(bf16[128,288]{0,1:T(8,128)(2,1)S(1)} %collective-permute-done.2), channel_id=1, source_target_pairs={{0,4},{1,5},{2,6},{3,7},{4,8},{5,9},{6,10},{7,11},{8,12},{9,13},{1... | collective-permute-start | bytes 221192 | tf_op jit(solution)/shard_map/ppermute | solution.py:31
  51.8 5.7 %collective-permute-start.4 = (bf16[128,288]{0,1:T(8,128)(2,1)S(1)}, bf16[128,288]{0,1:T(8,128)(2,1)S(1)}, u32[]{:S(2)}, u32[]{:S(2)}) collective-permute-start(bf16[128,288]{0,1:T(8,128)(2,1)S(1)} %collective-permute-done.3), channel_id=1, source_target_pairs={{0,4},{1,5},{2,6},{3,7},{4,8},{5,9},{6,10},{7,11},{8,12},{9,13},{1... | collective-permute-start | bytes 221192 | tf_op jit(solution)/shard_map/ppermute | solution.py:31
  63.2 5.9 %collective-permute-start.5 = (bf16[128,288]{0,1:T(8,128)(2,1)S(1)}, bf16[128,288]{0,1:T(8,128)(2,1)S(1)}, u32[]{:S(2)}, u32[]{:S(2)}) collective-permute-start(bf16[128,288]{0,1:T(8,128)(2,1)S(1)} %collective-permute-done.4), channel_id=1, source_target_pairs={{0,4},{1,5},{2,6},{3,7},{4,8},{5,9},{6,10},{7,11},{8,12},{9,13},{1... | collective-permute-start | bytes 221192 | tf_op jit(solution)/shard_map/ppermute | solution.py:31
  74.2 3.8 %collective-permute-start.6 = (bf16[128,288]{0,1:T(8,128)(2,1)S(1)}, bf16[128,288]{0,1:T(8,128)(2,1)S(1)}, u32[]{:S(2)}, u32[]{:S(2)}) collective-permute-start(bf16[128,288]{0,1:T(8,128)(2,1)S(1)} %collective-permute-done.5), channel_id=1, source_target_pairs={{0,4},{1,5},{2,6},{3,7},{4,8},{5,9},{6,10},{7,11},{8,12},{9,13},{1... | collective-permute-start | bytes 221192 | tf_op jit(solution)/shard_map/ppermute | solution.py:31
  89.8 27.4 %while.56 = (s32[]{:T(128)}, f32[2560]{0:T(1024)S(1)}, f32[2560]{0:T(1024)S(1)}, f32[2560,256]{1,0:T(8,128)S(1)}, bf16[1024,288]{1,0:T(8,128)(2,1)}, /*index=5*/...) while((s32[]{:T(128)}, f32[2560]{0:T(1024)S(1)}, ...), condition=%wide.region_5.6_spmd.clone, body=%wide.region_2.5_spmd.clone.sunk | while | flops 1439840768 | bytes 44730576 | solution.py:77
  90.5 5.7 %fusion.139 = (f32[2560]{0:T(1024)S(1)}, f32[512,2560]{1,0:T(8,128)}) fusion(pred[512]{0:T(512)(128)(4,1)S(1)} %fusion.138, bf16[2560,288]{1,0:T(8,128)(2,1)} %get-tuple-element.733, bf16[1024,288]{1,0:T(8,128)(2,1)} %get-tuple-element.732, s32[]{:T(128)S(6)} %select_n.166), kind=kOutput, calls=%fused_computation.53.clone.1 | convolution fusion | flops 758904320 | bytes 7612932 | tf_op jit(solution)/shard_map/while/body/eval_jaxpr/rw,kw->rk/dot_general | solution.py:63
  96.2 3.5 %fusion.140 = f32[2560]{0:T(1024)S(1)} fusion(f32[512,2560]{1,0:T(8,128)} %get-tuple-element.703, f32[2560]{0:T(1024)S(1)} %select_maximum_fusion.2, pred[512]{0:T(512)(128)(4,1)S(1)} %fusion.138), kind=kLoop, calls=%fused_computation.58.clone.1 | loop fusion | flops 3929600 | bytes 5263872 | tf_op jit(solution)/shard_map/while/body/eval_jaxpr/reduce_sum | solution.py:71
  103.9 5.7 %fusion.139 = (f32[2560]{0:T(1024)S(1)}, f32[512,2560]{1,0:T(8,128)}) fusion(pred[512]{0:T(512)(128)(4,1)S(1)} %fusion.138, bf16[2560,288]{1,0:T(8,128)(2,1)} %get-tuple-element.733, bf16[1024,288]{1,0:T(8,128)(2,1)} %get-tuple-element.732, s32[]{:T(128)S(6)} %select_n.166), kind=kOutput, calls=%fused_computation.53.clone.1 | convolution fusion | flops 758904320 | bytes 7612932 | tf_op jit(solution)/shard_map/while/body/eval_jaxpr/rw,kw->rk/dot_general | solution.py:63
  109.6 4.2 %fusion.140 = f32[2560]{0:T(1024)S(1)} fusion(f32[512,2560]{1,0:T(8,128)} %get-tuple-element.703, f32[2560]{0:T(1024)S(1)} %select_maximum_fusion.2, pred[512]{0:T(512)(128)(4,1)S(1)} %fusion.138), kind=kLoop, calls=%fused_computation.58.clone.1 | loop fusion | flops 3929600 | bytes 5263872 | tf_op jit(solution)/shard_map/while/body/eval_jaxpr/reduce_sum | solution.py:71
  117.3 12.7 %all-gather.8.cloned.1.call-done = bf16[4,4096,288]{1,2,0:T(8,128)(2,1)} async-done(((bf16[4,128,288]{1,2,0:T(8,128)(2,1)}), bf16[4,4096,288]{1,2,0:T(8,128)(2,1)}) %all-gather.8.cloned.1.call-update) | async-done | bytes 9437200 | tf_op jit(solution)/shard_map/all_gather | solution.py:147
  133.3 4.5 %copy.36 = bf16[1,4096,288]{2,1,0:T(8,128)(2,1)} copy(bf16[1,4096,288]{1,2,0:T(8,128)(2,1)} %constant_dynamic-slice_fusion) | data formatting | bytes 4718592 | tf_op jit(solution)/shard_map/jit(dynamic_index_in_dim)/dynamic_slice | solution.py:150
  137.8 62.4 %while.54 = (s32[]{:T(128)}, f32[2560]{0:T(1024)S(1)}, f32[2560]{0:T(1024)S(1)}, f32[2560,256]{1,0:T(8,128)S(1)}, bf16[4096,288]{1,0:T(8,128)(2,1)}, /*index=5*/...) while((s32[]{:T(128)}, f32[2560]{0:T(1024)S(1)}, ...), condition=%wide.region_9.10_spmd.clone, body=%wide.region_6.9_spmd.clone.sunk | while | flops 1439177728 | bytes 23759020 | solution.py:77
  200.1 19.1 %while.55 = (s32[]{:T(128)}, f32[2560]{0:T(1024)S(1)}, f32[2560]{0:T(1024)S(1)}, f32[2560,256]{1,0:T(8,128)S(1)}, bf16[1024,288]{0,1:T(8,128)(2,1)}, /*index=5*/...) while((s32[]{:T(128)}, f32[2560]{0:T(1024)S(1)}, ...), condition=%wide.region_14.15_spmd.clone, body=%wide.region_11.14_spmd.clone.sunk | while | flops 1447041536 | bytes 23730872 | solution.py:77
  200.6 4.0 %fusion.133 = (f32[2560]{0:T(1024)S(1)}, f32[512,2560]{1,0:T(8,128)S(1)}) fusion(s32[2560]{0:T(1024)S(1)} %lt.216, s32[512]{0:T(512)S(1)} %iota_add_fusion.5, pred[512]{0:T(512)(128)(4,1)S(1)} %broadcast_compare_fusion.2, bf16[2560,288]{1,0:T(8,128)(2,1)} %get-tuple-element.801, bf16[1024,288]{0,1:T(8,128)(2,1)} %get-tuple-element.800, ...), kind=kOutput, calls=%fused_computation.29.clone.1 | convolution fusion | flops 761525760 | bytes 7526916 | tf_op jit(solution)/shard_map/while/body/eval_jaxpr/rw,kw->rk/dot_general | solution.py:63
  210.1 4.0 %fusion.133 = (f32[2560]{0:T(1024)S(1)}, f32[512,2560]{1,0:T(8,128)S(1)}) fusion(s32[2560]{0:T(1024)S(1)} %lt.216, s32[512]{0:T(512)S(1)} %iota_add_fusion.5, pred[512]{0:T(512)(128)(4,1)S(1)} %broadcast_compare_fusion.2, bf16[2560,288]{1,0:T(8,128)(2,1)} %get-tuple-element.801, bf16[1024,288]{0,1:T(8,128)(2,1)} %get-tuple-element.800, ...), kind=kOutput, calls=%fused_computation.29.clone.1 | convolution fusion | flops 761525760 | bytes 7526916 | tf_op jit(solution)/shard_map/while/body/eval_jaxpr/rw,kw->rk/dot_general | solution.py:63
  223.8 3.9 %fusion.59 = bf16[128,2560]{1,0:T(8,128)(2,1)S(1)} fusion(bf16[128,1280]{0,1:T(8,128)(2,1)S(1)} %bitcast.101, bf16[1280,2560]{1,0:T(8,128)(2,1)} %param.34, bf16[128,2560]{1,0:T(8,128)(2,1)S(1)} %copy-done.4), kind=kOutput, calls=%fused_computation.79 | convolution fusion | flops 839843840 | bytes 8192000 | tf_op jit(solution)/shard_map/dot_general | solution.py:188
  229.4 16.0 %collective-permute-done.7 = bf16[128,2560]{1,0:T(8,128)(2,1)S(1)} collective-permute-done((bf16[128,2560]{1,0:T(8,128)(2,1)S(1)}, bf16[128,2560]{1,0:T(8,128)(2,1)S(1)}, u32[]{:S(2)}, u32[]{:S(2)}) %collective-permute-start.7) | collective-permute-done | bytes 655392 | tf_op jit(solution)/shard_map/ppermute | solution.py:21
  248.0 13.7 %collective-permute-done.8 = bf16[128,2560]{1,0:T(8,128)(2,1)S(1)} collective-permute-done((bf16[128,2560]{1,0:T(8,128)(2,1)S(1)}, bf16[128,2560]{1,0:T(8,128)(2,1)S(1)}, u32[]{:S(2)}, u32[]{:S(2)}) %collective-permute-start.8) | collective-permute-done | bytes 655392 | tf_op jit(solution)/shard_map/ppermute | solution.py:21
  269.3 6.8 %fusion.60 = f32[512,800]{0,1:T(8,128)} fusion(bf16[2560,800]{1,0:T(8,128)(2,1)} %all-gather.12.cloned.1.call-done, bf16[1024,2560]{1,0:T(8,128)(2,1)} %constant_dynamic-update-slice_fusion.8, s32[]{:T(128)S(6)} %select_n.106), kind=kOutput, calls=%fused_computation.82 | convolution fusion | flops 2097152000 | bytes 8847364 | tf_op jit(solution)/shard_map/dot_general | solution.py:199
  276.1 11.9 %convolution_convert_fusion = bf16[512,2560]{1,0:T(8,128)(2,1)} fusion(bf16[800,2560]{0,1:T(8,128)(2,1)} %all-gather.14.cloned.1.call-done, f32[512,800]{0,1:T(8,128)} %fusion.60, bf16[2560,800]{1,0:T(8,128)(2,1)} %all-gather.10.cloned.1.call-done, bf16[1024,2560]{1,0:T(8,128)(2,1)} %constant_dynamic-update-slice_fusion.8, s32[]{:T(128)S(6)} %select_n.106), kind=kOutput, calls=%fused_computation.77 | convolution fusion | flops 4198072320 | bytes 16056324 | tf_op jit(solution)/shard_map/dot_general | solution.py:205
  288.0 32.6 %reduce-scatter.2.cloned.1.call-done = bf16[128,2560]{1,0:T(8,128)(2,1)} async-done(((bf16[512,2560]{1,0:T(8,128)(2,1)}), bf16[128,2560]{1,0:T(8,128)(2,1)}) %reduce-scatter.2.cloned.1.call-update) | async-done | bytes 655376 | tf_op jit(solution)/shard_map/reduce_scatter | solution.py:210
  (197 shorter events, 146.6 us)
Async XLA Ops:
  7.2 29.4 %copy-start = (bf16[768,1920]{1,0:T(8,128)(2,1)S(1)}, bf16[768,1920]{1,0:T(8,128)(2,1)}, u32[]{:S(2)}) copy-start(bf16[768,1920]{1,0:T(8,128)(2,1)} %param.29) | copy-start | bytes 8847364
  7.2 80.5 %all-gather.6.cloned.1.call-start = ((), (), s32[]{:S(2)}) async-start(), calls=%async_computation.1 | async-start | bytes 6488064 | tf_op jit(solution)/shard_map/all_gather | solution.py:148
  7.9 122.1 %all-gather.8.cloned.1.call-start = ((), (), s32[]{:S(2)}) async-start(), calls=%async_computation.2 | async-start | bytes 9732096 | tf_op jit(solution)/shard_map/all_gather | solution.py:147
  8.7 260.6 %all-gather.12.cloned.1.call-start = ((), (), s32[]{:S(2)}) async-start(), calls=%async_computation.4 | async-start | bytes 4730880 | tf_op jit(solution)/shard_map/all_gather | solution.py:201
  9.4 266.7 %all-gather.10.cloned.1.call-start = ((), (), s32[]{:S(2)}) async-start(), calls=%async_computation.3 | async-start | bytes 4730880 | tf_op jit(solution)/shard_map/all_gather | solution.py:196
  10.0 266.1 %all-gather.14.cloned.1.call-start = ((), (), s32[]{:S(2)}) async-start(), calls=%async_computation.5 | async-start | bytes 4730880 | tf_op jit(solution)/shard_map/all_gather | solution.py:207
  22.5 9.6 %copy-start.9 = (bf16[768]{0:T(1024)(128)(2,1)S(1)}, bf16[768]{0:T(1024)(128)(2,1)}, u32[]{:S(2)}) copy-start(bf16[768]{0:T(1024)(128)(2,1)} %param.28) | copy-start | bytes 4612
  22.5 14.0 %copy-start.7 = (bf16[128,288]{0,1:T(8,128)(2,1)}, bf16[128,288]{0,1:T(8,128)(2,1)S(1)}, u32[]{:S(2)}) copy-start(bf16[128,288]{0,1:T(8,128)(2,1)S(1)} %pad_maximum_fusion.1) | copy-start | bytes 221188
  22.5 9.5 %collective-permute-start = (bf16[128,288]{0,1:T(8,128)(2,1)S(1)}, bf16[128,288]{0,1:T(8,128)(2,1)}, u32[]{:S(2)}, u32[]{:S(2)}) collective-permute-start(bf16[128,288]{0,1:T(8,128)(2,1)S(1)} %pad_maximum_fusion.1), channel_id=1, source_target_pairs={{0,4},{1,5},{2,6},{3,7},{4,8},{5,9},{6,10},{7,11},{8,12},{9,13},{1... | collective-permute-start | bytes 221192 | tf_op jit(solution)/shard_map/ppermute | solution.py:31
  28.8 291.8 %reduce-scatter.2.cloned.1.call-start = ((), (), s32[]{:S(2)}) async-start(), calls=%async_computation.6 | async-start | bytes 3276800 | tf_op jit(solution)/shard_map/reduce_scatter | solution.py:210
  32.0 6.7 %collective-permute-start.1 = (bf16[128,288]{0,1:T(8,128)(2,1)}, bf16[128,288]{0,1:T(8,128)(2,1)}, u32[]{:S(2)}, u32[]{:S(2)}) collective-permute-start(bf16[128,288]{0,1:T(8,128)(2,1)} %collective-permute-done), channel_id=1, source_target_pairs={{0,4},{1,5},{2,6},{3,7},{4,8},{5,9},{6,10},{7,11},{8,12},{9,13},{1... | collective-permute-start | bytes 221192 | tf_op jit(solution)/shard_map/ppermute | solution.py:31
  38.8 5.7 %collective-permute-start.2 = (bf16[128,288]{0,1:T(8,128)(2,1)}, bf16[128,288]{0,1:T(8,128)(2,1)S(1)}, u32[]{:S(2)}, u32[]{:S(2)}) collective-permute-start(bf16[128,288]{0,1:T(8,128)(2,1)} %collective-permute-done.1), channel_id=1, source_target_pairs={{0,4},{1,5},{2,6},{3,7},{4,8},{5,9},{6,10},{7,11},{8,12},{9,13},{1... | collective-permute-start | bytes 221192 | tf_op jit(solution)/shard_map/ppermute | solution.py:31
  44.5 7.3 %collective-permute-start.3 = (bf16[128,288]{0,1:T(8,128)(2,1)S(1)}, bf16[128,288]{0,1:T(8,128)(2,1)S(1)}, u32[]{:S(2)}, u32[]{:S(2)}) collective-permute-start(bf16[128,288]{0,1:T(8,128)(2,1)S(1)} %collective-permute-done.2), channel_id=1, source_target_pairs={{0,4},{1,5},{2,6},{3,7},{4,8},{5,9},{6,10},{7,11},{8,12},{9,13},{1... | collective-permute-start | bytes 221192 | tf_op jit(solution)/shard_map/ppermute | solution.py:31
  51.8 11.4 %collective-permute-start.4 = (bf16[128,288]{0,1:T(8,128)(2,1)S(1)}, bf16[128,288]{0,1:T(8,128)(2,1)S(1)}, u32[]{:S(2)}, u32[]{:S(2)}) collective-permute-start(bf16[128,288]{0,1:T(8,128)(2,1)S(1)} %collective-permute-done.3), channel_id=1, source_target_pairs={{0,4},{1,5},{2,6},{3,7},{4,8},{5,9},{6,10},{7,11},{8,12},{9,13},{1... | collective-permute-start | bytes 221192 | tf_op jit(solution)/shard_map/ppermute | solution.py:31
  63.2 11.0 %copy-start.8 = (bf16[2560]{0:T(1024)(128)(2,1)S(1)}, bf16[2560]{0:T(1024)(128)(2,1)}, u32[]{:S(2)}) copy-start(bf16[2560]{0:T(1024)(128)(2,1)} %param.35) | copy-start | bytes 15364
  63.2 11.0 %collective-permute-start.5 = (bf16[128,288]{0,1:T(8,128)(2,1)S(1)}, bf16[128,288]{0,1:T(8,128)(2,1)S(1)}, u32[]{:S(2)}, u32[]{:S(2)}) collective-permute-start(bf16[128,288]{0,1:T(8,128)(2,1)S(1)} %collective-permute-done.4), channel_id=1, source_target_pairs={{0,4},{1,5},{2,6},{3,7},{4,8},{5,9},{6,10},{7,11},{8,12},{9,13},{1... | collective-permute-start | bytes 221192 | tf_op jit(solution)/shard_map/ppermute | solution.py:31
  74.2 6.6 %collective-permute-start.6 = (bf16[128,288]{0,1:T(8,128)(2,1)S(1)}, bf16[128,288]{0,1:T(8,128)(2,1)S(1)}, u32[]{:S(2)}, u32[]{:S(2)}) collective-permute-start(bf16[128,288]{0,1:T(8,128)(2,1)S(1)} %collective-permute-done.5), channel_id=1, source_target_pairs={{0,4},{1,5},{2,6},{3,7},{4,8},{5,9},{6,10},{7,11},{8,12},{9,13},{1... | collective-permute-start | bytes 221192 | tf_op jit(solution)/shard_map/ppermute | solution.py:31
  96.2 4.0 %copy-start.2 = (f32[512,2560]{1,0:T(8,128)S(1)}, f32[512,2560]{1,0:T(8,128)}, u32[]{:S(2)}) copy-start(f32[512,2560]{1,0:T(8,128)} %get-tuple-element.703) | copy-start | bytes 15728644 | tf_op jit(solution)/shard_map/while
  109.6 4.8 %copy-start.2 = (f32[512,2560]{1,0:T(8,128)S(1)}, f32[512,2560]{1,0:T(8,128)}, u32[]{:S(2)}) copy-start(f32[512,2560]{1,0:T(8,128)} %get-tuple-element.703) | copy-start | bytes 15728644 | tf_op jit(solution)/shard_map/while
  227.7 39.6 %copy-start.3 = (bf16[128,2560]{1,0:T(8,128)(2,1)}, bf16[128,2560]{1,0:T(8,128)(2,1)S(1)}, u32[]{:S(2)}) copy-start(bf16[128,2560]{1,0:T(8,128)(2,1)S(1)} %fusion.59) | copy-start | bytes 1966084
  228.2 17.2 %collective-permute-start.7 = (bf16[128,2560]{1,0:T(8,128)(2,1)S(1)}, bf16[128,2560]{1,0:T(8,128)(2,1)S(1)}, u32[]{:S(2)}, u32[]{:S(2)}) collective-permute-start(bf16[128,2560]{1,0:T(8,128)(2,1)S(1)} %fusion.70), channel_id=1, source_target_pairs={{0,32},{32,64},{64,96},{96,0},{1,33},{33,65},{65,97},{97,1},{2,34}... | collective-permute-start | bytes 1966088 | tf_op jit(solution)/shard_map/ppermute | solution.py:21
  245.4 16.4 %collective-permute-start.8 = (bf16[128,2560]{1,0:T(8,128)(2,1)S(1)}, bf16[128,2560]{1,0:T(8,128)(2,1)S(1)}, u32[]{:S(2)}, u32[]{:S(2)}) collective-permute-start(bf16[128,2560]{1,0:T(8,128)(2,1)S(1)} %collective-permute-done.7), channel_id=1, source_target_pairs={{0,32},{32,64},{64,96},{96,0},{1,33},{33,65},{65,97},{97,1},{2,34}... | collective-permute-start | bytes 1966088 | tf_op jit(solution)/shard_map/ppermute | solution.py:21
  245.4 19.3 %collective-permute-start.9 = (bf16[128,2560]{1,0:T(8,128)(2,1)}, bf16[128,2560]{1,0:T(8,128)(2,1)S(1)}, u32[]{:S(2)}, u32[]{:S(2)}) collective-permute-start(bf16[128,2560]{1,0:T(8,128)(2,1)} %copy-done.6), channel_id=1, source_target_pairs={{0,96},{32,0},{64,32},{96,64},{1,97},{33,1},{65,33},{97,65},{2,98}... | collective-permute-start | bytes 1966088 | tf_op jit(solution)/shard_map/ppermute | solution.py:23
  276.1 46.8 %copy-start.1 = (bf16[768,1920]{1,0:T(8,128)(2,1)S(1)}, bf16[768,1920]{1,0:T(8,128)(2,1)}, u32[]{:S(2)}) copy-start(bf16[768,1920]{1,0:T(8,128)(2,1)} %param.29) | copy-start | bytes 8847364
  (3 other events, 6.6 us)
Sparse Core Ops, SparseCore 0:
  10.3 56.2 all-gather.5
  68.7 61.1 all-gather.7
  132.3 46.1 all-gather.11
  180.7 45.8 all-gather.9
  228.7 45.8 all-gather.13
  288.1 32.4 reduce-scatter.1
